TPU v7x, 32 devices: a whole 2x2x4 slice. The times are simulated.
32 devices in a mesh: groups: 2 (over x), ctx: 8 (over z, y), head: 2 (over core).
Axes of the slice: x: 2, y: 2, z: 4, core: 2. Of those that a mesh axis runs over, the one named last changes fastest.
Arguments:
- queries: bfloat16 [8192, 1024], P(('groups', 'ctx'), 'head'), parts along dimension 0, may hold values from -6 to 6
- keys: bfloat16 [8192, 1024], P(('groups', 'ctx'), 'head'), parts along dimension 0, may hold values from -6 to 6
- values: bfloat16 [8192, 2048], P(('groups', 'ctx'), 'head'), parts along dimension 0, may hold values from -30 to 30
- in_gate: float32 [4, 8192], P('head', ('groups', 'ctx')), parts along dimension 1, may hold values from -60 to 150
- forget_gate: float32 [4, 8192], P('head', ('groups', 'ctx')), parts along dimension 1, may hold values from -5 to 16
- w_out: bfloat16 [2048, 4096], P('head'), may hold values from -0.125 to 0.125
Outputs:
- layer_out: bfloat16 [8192, 4096], P(('groups', 'ctx', 'head')), parts along dimension 0
There are 2 independent parts, one for each index of `groups`. A program takes and returns all parts, laid end to end along the dimension named above; an argument that names none is the same for every part. Nothing has to cross between parts.
All inputs are finite; a program needn't handle non-finite values.
Results may differ from a plain program's by a relative error of at most 0.009.
Values may be sent and summed in bfloat16 or wider, within the bound.
No kernel may reach another device: no remote copies, remote signals or barrier semaphores. Data moves between devices by JAX's collectives and lax.ppermute only.
A program may use at most 192 MiB of HBM per device.

v0:
```python
import jax
import jax.numpy as jnp
from jax import lax
from jax.sharding import PartitionSpec as P

DK = 256
DV = 512


norm_epsilon = 1e-06
very_negative = -1e30


def prefix(part, axis, combine, identity):
    place = lax.axis_index(axis)
    gathered = jax.tree.map(lambda a: lax.all_gather(a, axis), part)
    state = jax.tree.map(lambda a, e: jnp.zeros_like(a) + jnp.asarray(e, a.dtype), part, identity)

    def one(turn, state):
        return combine(
            state, jax.tree.map(lambda a: lax.dynamic_index_in_dim(a, turn, 0, False), gathered)
        )

    return lax.fori_loop(0, place, one, state)


def join_states(earlier, latter):
    decay_first, max_first, state_first = earlier
    decay_second, max_second, state_second = latter
    joined = jnp.maximum(max_first + decay_second, max_second)
    merged = (
        jnp.exp(max_first + decay_second - joined)[:, None, None] * state_first
        + jnp.exp(max_second - joined)[:, None, None] * state_second
    )
    return (decay_first + decay_second, joined, merged)


def body(queries, keys, values, in_gate, forget_gate, w_out):
    row_count = queries.shape[0]
    head_count = in_gate.shape[0]
    score_scale = DK ** (-0.5)
    query_per_head = queries.reshape(row_count, head_count, DK)
    key_heads = keys.reshape(row_count, head_count, DK)
    value_per_head = values.reshape(row_count, head_count, DV)
    running = jnp.cumsum(jax.nn.log_sigmoid(forget_gate), axis=1)
    decay_total = running[:, -1]
    tail_log = decay_total[:, None] - running + in_gate
    local_max = jnp.max(tail_log, axis=1)
    key_scaled_rows = (key_heads * jnp.exp(tail_log - local_max[:, None]).T[:, :, None]).astype(
        jnp.bfloat16
    )
    segment_state = jnp.einsum(
        "ben,bet->ent", key_scaled_rows, value_per_head, preferred_element_type=jnp.float32
    )
    identity = (
        jnp.zeros((head_count,), jnp.float32),
        jnp.full((head_count,), very_negative, jnp.float32),
        jnp.zeros((head_count, DK, DV), jnp.float32),
    )
    scanned = prefix((decay_total, local_max, segment_state), "ctx", join_states, identity)
    prev_max = scanned[1]
    previous_state = scanned[2]
    causal = jnp.arange(row_count)[:, None] >= jnp.arange(row_count)[None, :]
    scores = (
        jnp.einsum("thk,shk->hts", query_per_head, key_heads, preferred_element_type=jnp.float32)
        * score_scale
    )
    log_weight = jnp.where(
        causal[None], running[:, :, None] - running[:, None, :] + in_gate[:, None, :], -jnp.inf
    )
    carry_log = running + prev_max[:, None]
    stabilizer = jnp.maximum(jnp.max(log_weight, axis=2), carry_log)
    weights = (jnp.exp(log_weight - stabilizer[:, :, None]) * scores).astype(jnp.bfloat16)
    local_term = jnp.einsum(
        "hts,shv->thv", weights, value_per_head, preferred_element_type=jnp.float32
    )
    carryover_term = jnp.einsum(
        "raq,aqy->ray",
        query_per_head.astype(jnp.float32),
        previous_state,
        precision=lax.Precision.HIGHEST,
    )
    hidden = (
        local_term + carryover_term * (score_scale * jnp.exp(carry_log - stabilizer)).T[:, :, None]
    )
    normed = hidden * lax.rsqrt(jnp.mean(hidden * hidden, axis=2, keepdims=True) + norm_epsilon)
    mixed = normed.astype(jnp.bfloat16).reshape(row_count, head_count * DV)
    return lax.psum_scatter(
        jnp.dot(mixed, w_out, preferred_element_type=jnp.float32).astype(jnp.bfloat16),
        "head",
        scatter_dimension=0,
        tiled=True,
    )


def solution(mesh):
    return jax.shard_map(
        body,
        mesh=mesh,
        in_specs=(
            P(("groups", "ctx"), "head"),
            P(("groups", "ctx"), "head"),
            P(("groups", "ctx"), "head"),
            P("head", ("groups", "ctx")),
            P("head", ("groups", "ctx")),
            P("head", None),
        ),
        out_specs=P(("groups", "ctx", "head"), None),
        check_vma=False,
    )
```

profile of v0, /device:TPU:29, one launch (start us, length us, event | category | flops | bytes accessed | tf_op | source)
XLA Modules:
  0.0 185.0 jit_solution(17522230162561934685)
XLA Ops:
  6.5 0.8 fusion.23
  7.3 0.6 reduce-window.6
  8.0 0.2 slice_reduce_fusion
  8.1 0.2 reduce-window.9
  8.4 0.2 slice_reduce_fusion.1
  8.6 1.5 copy.26
  10.1 0.2 copy.25
  10.3 0.2 fusion.27
  10.6 1.4 fusion.15
  12.1 0.6 dynamic-slice
  13.3 0.2 dynamic-update-slice.1
  13.5 0.2 dynamic-update-slice
  13.7 13.7 %all-reduce.2 = (f32[16]{0:T(128)S(1)}, f32[16]{0:T(128)S(1)}) all-reduce(f32[16]{0:T(128)S(1)} %dynamic-update-slice, f32[16]{0:T(128)S(1)} %dynamic-update-slice.1), channel_id=2, replica_groups=mesh['groups'=2,'ctx'=8,'head'=2] {'ctx'}, use_global_device_ids=true, to_apply=%add | all-reduce | flops 32 | bytes 256
  27.4 0.1 reshape.103
  27.6 0.1 iota_compare_fusion
  27.7 0.7 fusion.6
  28.3 107.2 %all-gather.5.cloned.1.call-done = f32[16,256,512]{2,1,0:T(8,128)} async-done(((f32[2,256,512]{2,1,0:T(8,128)}), f32[16,256,512]{2,1,0:T(8,128)}) %all-gather.5.cloned.1.call-update) | async-done | bytes 8388624 | tf_op jit(solution)/shard_map/all_gather | solution.py:16
  135.5 0.1 broadcast_in_dim.16
  135.7 12.5 %while.14 = (s32[]{:T(128)}, f32[2]{0:T(128)S(1)}, f32[2,256,512]{2,1,0:T(8,128)S(1)}, s32[]{:T(128)}, f32[8,2]{1,0:T(8,128)S(1)}, /*index=5*/f32[8,2]{1,0:T(8,1...) while((s32[]{:T(128)}, f32[2]{0:T(128)S(1)}, f32[2,256,512]{2,1,0:T(8,128)S(1)}, ...), condition=%wide.region_5.6_spmd, body=%wide.region_4.5_spmd.sunk | while | flops 786445 | bytes 3145955 | solution.py:24
  135.7 1.8 fusion.35
  137.6 1.7 fusion.35
  139.3 1.7 fusion.35
  141.1 1.7 fusion.35
  142.9 1.7 fusion.35
  144.7 1.7 fusion.35
  146.5 1.7 fusion.35
  148.2 0.1 multiply_bitcast_fusion
  148.3 2.7 %fusion.7 = f32[2,512,512]{1,2,0:T(8,128)} fusion(bf16[512,2,512]{0,2,1:T(8,128)(2,1)S(1)} %bitcast.71, bf16[512,2,256]{0,2,1:T(8,128)(2,1)S(1)} %bitcast.74, f32[2,512]{1,0:T(2,128)S(1)} %get-tuple-element.85, f32[2,512]{1,0:T(2,128)S(1)} %copy-done.2, f32[2,512]{1,0:T(2,128)S(1)} %bitcast.80, pred[512,512]{1,0:T(8,128)(4,1)S(1)} %iota_compare_fusion, ...), kind=kOutput, calls=%fused_computation.18 | convolution fusion | flops 808976384 | bytes 4468736 | tf_op jit(solution)/shard_map/hts,shv->thv/dot_general | solution.py:74
  151.0 3.6 %multiply_reduce_fusion = (f32[512,2]{0,1:T(2,128)S(1)}, f32[512,2,512]{0,2,1:T(8,128)S(1)}) fusion(f32[512,2]{0,1:T(2,128)S(1)} %get-tuple-element.84, f32[2,256,512]{2,1,0:T(8,128)S(1)} %get-tuple-element.65, bf16[64,2,8,256]{3,2,1,0:T(8,128)(2,1)S(1)} %bitcast.77, f32[2,512,512]{1,2,0:T(8,128)} %fusion.7), kind=kOutput, calls=%fused_computation.14 | convolution fusion | flops 1612708864 | bytes 5775360 | tf_op jit(solution)/shard_map/raq,aqy->ray/dot_general | solution.py:77
  154.6 0.3 multiply_convert_fusion
  154.9 9.5 %convolution_convert_fusion = bf16[512,4096]{1,0:T(8,128)(2,1)} fusion(bf16[512,1024]{0,1:T(8,128)(2,1)S(1)} %bitcast.75, bf16[1024,4096]{1,0:T(8,128)(2,1)} %param.13), kind=kOutput, calls=%fused_computation.10 | convolution fusion | flops 4297064448 | bytes 13631488 | tf_op jit(solution)/shard_map/dot_general | solution.py:89
  164.4 13.7 %reduce-scatter.2.cloned.1.call-done = bf16[256,4096]{1,0:T(8,128)(2,1)} async-done(((bf16[512,4096]{1,0:T(8,128)(2,1)}), bf16[256,4096]{1,0:T(8,128)(2,1)}) %reduce-scatter.2.cloned.1.call-update) | async-done | bytes 2097168 | tf_op jit(solution)/shard_map/reduce_scatter | solution.py:88
  (35 shorter events, 0.6 us)
Async XLA Ops:
  6.5 3.5 %copy-start = (bf16[512,512]{1,0:T(8,128)(2,1)S(1)}, bf16[512,512]{1,0:T(8,128)(2,1)}, u32[]{:S(2)}) copy-start(bf16[512,512]{1,0:T(8,128)(2,1)} %param.9) | copy-start | bytes 1572868
  6.5 3.8 %copy-start.2 = (f32[2,512]{1,0:T(2,128)S(1)}, f32[2,512]{1,0:T(2,128)}, u32[]{:S(2)}) copy-start(f32[2,512]{1,0:T(2,128)} %param.11) | copy-start | bytes 12292
  6.5 129.0 %all-gather.5.cloned.1.call-start = ((), (), s32[]{:S(2)}) async-start(), calls=%async_computation.2 | async-start | bytes 9437184 | tf_op jit(solution)/shard_map/all_gather | solution.py:16
  10.3 1.8 copy-start.3
  12.1 166.1 %reduce-scatter.2.cloned.1.call-start = ((), (), s32[]{:S(2)}) async-start(), calls=%async_computation.1 | async-start | bytes 6291456 | tf_op jit(solution)/shard_map/reduce_scatter | solution.py:88
  135.6 12.6 %copy-start.1 = (bf16[512,512]{1,0:T(8,128)(2,1)S(1)}, bf16[512,512]{1,0:T(8,128)(2,1)}, u32[]{:S(2)}) copy-start(bf16[512,512]{1,0:T(8,128)(2,1)} %param.8) | copy-start | bytes 1572868
Sparse Core Ops, SparseCore 0:
  12.2 123.2 all-gather.4
  164.5 13.5 reduce-scatter.1
where the time goes:
time: 186 us; the launch traced here: 185 us
  waiting for transfers between devices  121 us (65%)
  matrix products  17.2 us (9%)
  other arithmetic  15.3 us (8%)
  between operations  14.1 us (8%)
  blocking collectives  13.7 us (7%)
  local copies, waits for them, and re-layouts  3.38 us (2%)
    all_gather x1, waiting for transfers between devices, prefix(): gathered = jax.tree.map(lambda a: lax.all_gather(a, axis), part)  107 us
    unnamed x1, blocking collectives  13.7 us
    reduce_scatter x1, waiting for transfers between devices, body(): lax.psum_scatter(jnp.dot(mixed, w_out, preferred_element_type=jnp.float32...  13.7 us
    add x7, other arithmetic, join_states(): jnp.exp(max_first + decay_second - joined)[:, None, None] * state_first  12.1 us
    dot_general x1, matrix products, body(): jnp.dot(mixed, w_out, preferred_element_type=jnp.float32)  9.48 us
  transfers between devices with their start and end apart: 2, of which 2 were waited for; matrix products, arithmetic and copies ran while one was open for 1% of the time, Pallas kernels for 0%

commit v1 on v0

v1 whole, which is shorter than its diff:
```python
import jax
import jax.numpy as jnp
from jax import lax
from jax.sharding import PartitionSpec as P

DK = 256
DV = 512


norm_epsilon = 1e-06
very_negative = -1e30


def join_states(earlier, latter):
    decay_first, max_first, state_first = earlier
    decay_second, max_second, state_second = latter
    joined = jnp.maximum(max_first + decay_second, max_second)
    merged = (
        jnp.exp(max_first + decay_second - joined)[:, None, None] * state_first
        + jnp.exp(max_second - joined)[:, None, None] * state_second
    )
    return (decay_first + decay_second, joined, merged)


def exclusive_prefix(own, ctx_count):
    place = lax.axis_index("ctx")
    decay, top, state = own
    head_count = decay.shape[0]
    covered = (decay, top, state)
    earlier = (
        jnp.zeros((head_count,), jnp.float32),
        jnp.full((head_count,), very_negative, jnp.float32),
        jnp.zeros_like(state),
    )
    shift = 1
    while shift < ctx_count:
        pairs = [(i, i + shift) for i in range(ctx_count - shift)]
        scalars = lax.ppermute(jnp.stack([covered[0], covered[1]]), "ctx", pairs)
        got_state = lax.ppermute(covered[2], "ctx", pairs)
        valid = place >= shift
        got = (
            jnp.where(valid, scalars[0], 0.0),
            jnp.where(valid, scalars[1], very_negative),
            got_state,
        )
        earlier = join_states(got, earlier)
        if 2 * shift < ctx_count:
            covered = join_states(got, covered)
        shift *= 2
    return earlier


def make_body(ctx_count, head_axis_count):
    def body(queries, keys, values, in_gate, forget_gate, w_out):
        row_count = queries.shape[0]
        head_count = in_gate.shape[0]
        score_scale = DK ** (-0.5)
        query_per_head = queries.reshape(row_count, head_count, DK)
        key_heads = keys.reshape(row_count, head_count, DK)
        value_per_head = values.reshape(row_count, head_count, DV)
        running = jnp.cumsum(jax.nn.log_sigmoid(forget_gate), axis=1)
        decay_total = running[:, -1]
        tail_log = decay_total[:, None] - running + in_gate
        local_max = jnp.max(tail_log, axis=1)
        key_scaled_rows = (
            key_heads * jnp.exp(tail_log - local_max[:, None]).T[:, :, None]
        ).astype(jnp.bfloat16)
        segment_state = jnp.einsum(
            "ben,bet->ent", key_scaled_rows, value_per_head, preferred_element_type=jnp.float32
        )
        scanned = exclusive_prefix((decay_total, local_max, segment_state), ctx_count)
        prev_max = scanned[1]
        previous_state = scanned[2]
        causal = jnp.arange(row_count)[:, None] >= jnp.arange(row_count)[None, :]
        scores = (
            jnp.einsum("thk,shk->hts", query_per_head, key_heads, preferred_element_type=jnp.float32)
            * score_scale
        )
        log_weight = jnp.where(
            causal[None], running[:, :, None] - running[:, None, :] + in_gate[:, None, :], -jnp.inf
        )
        carry_log = running + prev_max[:, None]
        stabilizer = jnp.maximum(jnp.max(log_weight, axis=2), carry_log)
        weights = (jnp.exp(log_weight - stabilizer[:, :, None]) * scores).astype(jnp.bfloat16)
        local_term = jnp.einsum(
            "hts,shv->thv", weights, value_per_head, preferred_element_type=jnp.float32
        )
        carryover_term = jnp.einsum(
            "raq,aqy->ray",
            query_per_head.astype(jnp.float32),
            previous_state,
            precision=lax.Precision.HIGHEST,
        )
        hidden = (
            local_term
            + carryover_term * (score_scale * jnp.exp(carry_log - stabilizer)).T[:, :, None]
        )
        normed = hidden * lax.rsqrt(jnp.mean(hidden * hidden, axis=2, keepdims=True) + norm_epsilon)
        mixed = normed.astype(jnp.bfloat16).reshape(row_count, head_count * DV)
        if head_axis_count != 2:
            return lax.psum_scatter(
                jnp.dot(mixed, w_out, preferred_element_type=jnp.float32).astype(jnp.bfloat16),
                "head",
                scatter_dimension=0,
                tiled=True,
            )
        core = lax.axis_index("head")
        half = row_count // 2
        peer_rows = lax.dynamic_slice_in_dim(mixed, (1 - core) * half, half, 0)
        own_rows = lax.dynamic_slice_in_dim(mixed, core * half, half, 0)
        peer_part = jnp.dot(peer_rows, w_out, preferred_element_type=jnp.float32).astype(
            jnp.bfloat16
        )
        received = lax.ppermute(peer_part, "head", [(0, 1), (1, 0)])
        own_part = jnp.dot(own_rows, w_out, preferred_element_type=jnp.float32)
        return (own_part + received.astype(jnp.float32)).astype(jnp.bfloat16)

    return body


def solution(mesh):
    return jax.shard_map(
        make_body(mesh.shape["ctx"], mesh.shape["head"]),
        mesh=mesh,
        in_specs=(
            P(("groups", "ctx"), "head"),
            P(("groups", "ctx"), "head"),
            P(("groups", "ctx"), "head"),
            P("head", ("groups", "ctx")),
            P("head", ("groups", "ctx")),
            P("head", None),
        ),
        out_specs=P(("groups", "ctx", "head"), None),
        check_vma=False,
    )
```

time: 186 us -> 139 us (0.75)
  waiting for transfers between devices: 121 us -> 99.3 us
  between operations: 14.1 us -> 0.22 us
  blocking collectives: 13.7 us -> 0 us
  other arithmetic: 15.3 us -> 5.33 us
  starting transfers between devices: 0.04 us -> 8.37 us
  matrix products: 17.2 us -> 23.9 us
    all_gather x1 -> x0, waiting for transfers between devices: 107 us -> none  [prefix(): gathered = jax.tree.map(lambda a: lax.all_gather(a, axis), part)]
    ppermute x0 -> x7, waiting for transfers between devices: none -> 99.3 us  [the longest x3 66.7 us: exclusive_prefix(): got_state = lax.ppermute(covered[2], 'ctx', pairs)]
    unnamed x1 -> x0, blocking collectives: 13.7 us -> none
    reduce_scatter x1 -> x0, waiting for transfers between devices: 13.7 us -> none  [body(): lax.psum_scatter(jnp.dot(mixed, w_out, preferred_element_type=jnp.float32...]
    add x7 -> x2, other arithmetic: 12.1 us -> 1.58 us  [join_states(): jnp.exp(max_first + decay_second - joined)[:, None, None] * state_first]
    ppermute x0 -> x7, starting transfers between devices: none -> 8.37 us  [the longest x3 4 us: exclusive_prefix(): got_state = lax.ppermute(covered[2], 'ctx', pairs)]
    dot_general x1 -> x2, matrix products: 9.48 us -> 14.2 us  [the longest x1 7.12 us: body(): own_part = jnp.dot(own_rows, w_out, preferred_element_type=jnp.float32)]
  transfers between devices with their start and end apart: 2 -> 7, of which waited for: 2 -> 5; matrix products, arithmetic and copies ran while one was open for 1% -> 6% of each run, Pallas kernels for 0% -> 0%
where the time goes in v1:
time: 139 us
  waiting for transfers between devices  99.3 us (71%)
  matrix products  23.9 us (17%)
  starting transfers between devices  8.37 us (6%)
  other arithmetic  5.33 us (4%)
  local copies, waits for them, and re-layouts  1.63 us (1%)
    ppermute x3, waiting for transfers between devices, exclusive_prefix(): got_state = lax.ppermute(covered[2], 'ctx', pairs)  66.7 us
    ppermute x3, waiting for transfers between devices, exclusive_prefix(): scalars = lax.ppermute(jnp.stack([covered[0], covered[1]]), 'ctx', pairs)  28.7 us
    dot_general x1, matrix products, body(): own_part = jnp.dot(own_rows, w_out, preferred_element_type=jnp.float32)  7.12 us
    dot_general x1, matrix products, body(): jnp.dot(peer_rows, w_out, preferred_element_type=jnp.float32)  7.09 us
    dot_general x1, matrix products, body(): jnp.einsum('raq,aqy->ray', query_per_head.astype(jnp.float32), previous_s...  4.05 us
    ppermute x1, waiting for transfers between devices, body(): received = lax.ppermute(peer_part, 'head', [(0, 1), (1, 0)])  4 us
    ppermute x3, starting transfers between devices, exclusive_prefix(): got_state = lax.ppermute(covered[2], 'ctx', pairs)  4 us
    dot_general x1, matrix products, body(): jnp.einsum('hts,shv->thv', weights, value_per_head, preferred_element_typ...  3.95 us
  transfers between devices with their start and end apart: 7, of which 5 were waited for; matrix products, arithmetic and copies ran while one was open for 6% of the time, Pallas kernels for 0%

profile of v1, /device:TPU:29, one launch (start us, length us, event | category | flops | bytes accessed | tf_op | source)
XLA Modules:
  0.0 138.7 jit_solution(18384885856232793145)
XLA Ops:
  0.0 0.7 fusion.41
  0.7 0.6 reduce-window.6
  1.4 0.2 slice_reduce_fusion
  1.5 0.2 reduce-window.9
  1.7 0.1 add_bitcast_fusion
  1.8 0.2 slice_reduce_fusion.1
  2.0 0.9 fusion.56
  2.8 1.3 collective-permute-start
  4.1 1.3 copy.18
  5.4 0.1 exponential_bitcast_fusion
  5.5 1.7 %fusion.4 = f32[2,256,512]{2,1,0:T(8,128)S(1)} fusion(bf16[64,2,8,512]{3,2,1,0:T(8,128)(2,1)} %bitcast.108, bf16[512,2,256]{0,2,1:T(8,128)(2,1)S(1)} %bitcast.106, f32[512,2]{0,1:T(2,128)S(1)} %exponential_bitcast_fusion), kind=kOutput, calls=%fused_computation.11 | convolution fusion | flops 269221888 | bytes 2625536 | tf_op jit(solution)/shard_map/ben,bet->ent/dot_general | solution.py:68
  7.2 1.3 collective-permute-start.3
  8.5 1.3 collective-permute-start.1
  9.8 24.7 %collective-permute-done.1 = f32[2,2]{1,0:T(2,128)S(1)} collective-permute-done((f32[2,2]{1,0:T(2,128)S(1)}, f32[2,2]{1,0:T(2,128)S(1)}, u32[]{:S(2)}, u32[]{:S(2)}) %collective-permute-start.1) | collective-permute-done | bytes 48 | tf_op jit(solution)/shard_map/ppermute | solution.py:38
  34.6 1.3 collective-permute-start.2
  35.9 3.9 %collective-permute-done.2 = f32[2,2]{1,0:T(2,128)S(1)} collective-permute-done((f32[2,2]{1,0:T(2,128)S(1)}, f32[2,2]{1,0:T(2,128)S(1)}, u32[]{:S(2)}, u32[]{:S(2)}) %collective-permute-start.2) | collective-permute-done | bytes 48 | tf_op jit(solution)/shard_map/ppermute | solution.py:38
  39.9 0.3 multiply_add_fusion.1
  40.2 1.4 %collective-permute-start.4 = (f32[2,256,512]{2,1,0:T(8,128)S(1)}, f32[2,256,512]{2,1,0:T(8,128)S(1)}, u32[]{:S(2)}, u32[]{:S(2)}) collective-permute-start(f32[2,256,512]{2,1,0:T(8,128)S(1)} %multiply_add_fusion.1), channel_id=1, source_target_pairs={{0,4},{2,6},{4,8},{6,10},{8,12},{10,14},{1,5},{3,7},{5,9},{7,11},{... | collective-permute-start | bytes 3145736 | tf_op jit(solution)/shard_map/ppermute | solution.py:39
  41.6 22.2 %collective-permute-done.4 = f32[2,256,512]{2,1,0:T(8,128)S(1)} collective-permute-done((f32[2,256,512]{2,1,0:T(8,128)S(1)}, f32[2,256,512]{2,1,0:T(8,128)S(1)}, u32[]{:S(2)}, u32[]{:S(2)}) %collective-permute-start.4) | collective-permute-done | bytes 1048608 | tf_op jit(solution)/shard_map/ppermute | solution.py:39
  63.9 1.3 multiply_add_fusion
  65.1 1.3 collective-permute-start.5
  66.4 0.1 iota_compare_fusion
  66.5 0.7 fusion.1
  67.2 0.1 multiply_bitcast_fusion
  67.3 4.0 %fusion.2 = f32[2,512,512]{1,2,0:T(8,128)} fusion(bf16[512,2,256]{0,2,1:T(8,128)(2,1)S(1)} %bitcast.107, f32[2,512]{1,0:T(2,128)S(1)} %get-tuple-element.14, f32[2,512]{1,0:T(2,128)S(1)} %copy-done.1, f32[2,512]{1,0:T(2,128)S(1)} %bitcast.114, pred[512,512]{1,0:T(8,128)(4,1)S(1)} %iota_compare_fusion, bf16[64,2,8,512]{3,2,1,0:T(8,128)(2,1)} %bitcast.109, ...), kind=kOutput, calls=%fused_computation.9 | convolution fusion | flops 808976384 | bytes 4468736 | tf_op jit(solution)/shard_map/hts,shv->thv/dot_general | solution.py:85
  71.2 44.4 %collective-permute-done.5 = f32[2,256,512]{2,1,0:T(8,128)} collective-permute-done((f32[2,256,512]{2,1,0:T(8,128)}, f32[2,256,512]{2,1,0:T(8,128)}, u32[]{:S(2)}, u32[]{:S(2)}) %collective-permute-start.5) | collective-permute-done | bytes 1048608 | tf_op jit(solution)/shard_map/ppermute | solution.py:39
  115.7 4.0 %multiply_reduce_fusion = (f32[512,2]{0,1:T(2,128)S(1)}, f32[512,2,512]{0,2,1:T(8,128)S(1)}) fusion(f32[512,2]{0,1:T(2,128)S(1)} %get-tuple-element.13, bf16[64,2,8,256]{3,2,1,0:T(8,128)(2,1)S(1)} %bitcast.111, f32[2,256,512]{2,1,0:T(8,128)S(1)} %collective-permute-done.3, f32[2,256,512]{2,1,0:T(8,128)S(1)} %collective-permute-done.4, ...), kind=kOutput, calls=%fused_computation.5 | convolution fusion | flops 1614806016 | bytes 7872560 | tf_op jit(solution)/shard_map/raq,aqy->ray/dot_general | solution.py:88
  119.7 0.3 multiply_convert_fusion
  120.0 7.1 %convolution_convert_fusion = bf16[256,4096]{1,0:T(8,128)(2,1)} fusion(bf16[1024,4096]{1,0:T(8,128)(2,1)} %param.11, bf16[512,1024]{0,1:T(8,128)(2,1)S(1)} %bitcast.104, s32[]{:T(128)S(6)} %select_n.184), kind=kOutput, calls=%fused_computation | convolution fusion | flops 2148532224 | bytes 11010052 | tf_op jit(solution)/shard_map/dot_general | solution.py:111
  127.1 0.5 collective-permute-start.6
  127.6 4.0 %collective-permute-done.6 = bf16[256,4096]{1,0:T(8,128)(2,1)S(1)} collective-permute-done((bf16[256,4096]{1,0:T(8,128)(2,1)}, bf16[256,4096]{1,0:T(8,128)(2,1)S(1)}, u32[]{:S(2)}, u32[]{:S(2)}) %collective-permute-start.6) | collective-permute-done | bytes 2097184 | tf_op jit(solution)/shard_map/ppermute | solution.py:114
  131.6 7.1 %add_convert_fusion = bf16[256,4096]{1,0:T(8,128)(2,1)} fusion(bf16[256,4096]{1,0:T(8,128)(2,1)S(1)} %collective-permute-done.6, bf16[1024,4096]{1,0:T(8,128)(2,1)} %param.11, bf16[512,1024]{0,1:T(8,128)(2,1)S(1)} %bitcast.105, s32[]{:T(128)S(6)} %select_n.183), kind=kOutput, calls=%fused_computation.1 | convolution fusion | flops 2150629376 | bytes 13107204 | tf_op jit(solution)/shard_map/dot_general | solution.py:115
  (18 shorter events, 0.1 us)
Async XLA Ops:
  2.8 5.6 %collective-permute-start = (f32[2,2]{1,0:T(2,128)S(1)}, f32[2,2]{1,0:T(2,128)S(1)}, u32[]{:S(2)}, u32[]{:S(2)}) collective-permute-start(f32[2,2]{1,0:T(2,128)S(1)} %pad_maximum_fusion), channel_id=1, source_target_pairs={{0,2},{2,4},{4,6},{6,8},{8,10},{10,12},{12,14},{1,3},{3,5},{5,7},{... | collective-permute-start | bytes 56 | tf_op jit(solution)/shard_map/ppermute | solution.py:38
  7.2 32.7 %collective-permute-start.3 = (f32[2,256,512]{2,1,0:T(8,128)S(1)}, f32[2,256,512]{2,1,0:T(8,128)S(1)}, u32[]{:S(2)}, u32[]{:S(2)}) collective-permute-start(f32[2,256,512]{2,1,0:T(8,128)S(1)} %fusion.4), channel_id=1, source_target_pairs={{0,2},{2,4},{4,6},{6,8},{8,10},{10,12},{12,14},{1,3},{3,5},{5,7},{... | collective-permute-start | bytes 3145736 | tf_op jit(solution)/shard_map/ppermute | solution.py:39
  8.5 26.0 %collective-permute-start.1 = (f32[2,2]{1,0:T(2,128)S(1)}, f32[2,2]{1,0:T(2,128)S(1)}, u32[]{:S(2)}, u32[]{:S(2)}) collective-permute-start(f32[2,2]{1,0:T(2,128)S(1)} %pad_maximum_fusion.1), channel_id=1, source_target_pairs={{0,4},{2,6},{4,8},{6,10},{8,12},{10,14},{1,5},{3,7},{5,9},{7,11},{... | collective-permute-start | bytes 56 | tf_op jit(solution)/shard_map/ppermute | solution.py:38
  34.6 5.2 %collective-permute-start.2 = (f32[2,2]{1,0:T(2,128)S(1)}, f32[2,2]{1,0:T(2,128)S(1)}, u32[]{:S(2)}, u32[]{:S(2)}) collective-permute-start(f32[2,2]{1,0:T(2,128)S(1)} %pad_maximum_fusion.2), channel_id=1, source_target_pairs={{0,8},{2,10},{4,12},{6,14},{1,9},{3,11},{5,13},{7,15},{16,24},{18,... | collective-permute-start | bytes 56 | tf_op jit(solution)/shard_map/ppermute | solution.py:38
  40.2 26.4 %copy-start.1 = (f32[2,512]{1,0:T(2,128)S(1)}, f32[2,512]{1,0:T(2,128)}, u32[]{:S(2)}) copy-start(f32[2,512]{1,0:T(2,128)} %param.9) | copy-start | bytes 12292
  40.2 27.1 %copy-start = (bf16[512,512]{1,0:T(8,128)(2,1)S(1)}, bf16[512,512]{1,0:T(8,128)(2,1)}, u32[]{:S(2)}) copy-start(bf16[512,512]{1,0:T(8,128)(2,1)} %param.6) | copy-start | bytes 1572868
  40.2 23.7 %collective-permute-start.4 = (f32[2,256,512]{2,1,0:T(8,128)S(1)}, f32[2,256,512]{2,1,0:T(8,128)S(1)}, u32[]{:S(2)}, u32[]{:S(2)}) collective-permute-start(f32[2,256,512]{2,1,0:T(8,128)S(1)} %multiply_add_fusion.1), channel_id=1, source_target_pairs={{0,4},{2,6},{4,8},{6,10},{8,12},{10,14},{1,5},{3,7},{5,9},{7,11},{... | collective-permute-start | bytes 3145736 | tf_op jit(solution)/shard_map/ppermute | solution.py:39
  65.1 50.5 %collective-permute-start.5 = (f32[2,256,512]{2,1,0:T(8,128)}, f32[2,256,512]{2,1,0:T(8,128)}, u32[]{:S(2)}, u32[]{:S(2)}) collective-permute-start(f32[2,256,512]{2,1,0:T(8,128)} %multiply_add_fusion), channel_id=1, source_target_pairs={{0,8},{2,10},{4,12},{6,14},{1,9},{3,11},{5,13},{7,15},{16,24},{18,... | collective-permute-start | bytes 3145736 | tf_op jit(solution)/shard_map/ppermute | solution.py:39
  127.1 4.5 %collective-permute-start.6 = (bf16[256,4096]{1,0:T(8,128)(2,1)}, bf16[256,4096]{1,0:T(8,128)(2,1)S(1)}, u32[]{:S(2)}, u32[]{:S(2)}) collective-permute-start(bf16[256,4096]{1,0:T(8,128)(2,1)} %convolution_convert_fusion), channel_id=1, source_target_pairs={{0,1},{1,0},{2,3},{3,2},{4,5},{5,4},{6,7},{7,6},{8,9},{9,8},{10,11... | collective-permute-start | bytes 6291464 | tf_op jit(solution)/shard_map/ppermute | solution.py:114
